TPU v7x, 512 devices: a whole 4x8x8 slice. The times are simulated.
512 devices in a mesh: expert: 64 (over x, z, core), group: 8 (over y).
Axes of the slice: x: 4, y: 8, z: 8, core: 2. Of those that a mesh axis runs over, the one named last changes fastest.
Arguments:
- tokens: bfloat16 [4096, 4096], P('expert', 'group'), may hold values from -6 to 6
- gate_weight: bfloat16 [64, 1536, 4096], P('expert', 'group'), may hold values from -0.09375 to 0.09375
- up_weight: bfloat16 [64, 1536, 4096], P('expert', 'group'), may hold values from -0.09375 to 0.09375
- down_weight: bfloat16 [64, 1536, 4096], P('expert', 'group'), may hold values from -0.15625 to 0.15625
- expert_ids: int32 [4096, 8], P('expert'), may hold values from 0 to 63, all different within a row; in each aligned block of 64 rows (0 to 63, 64 to 127, ...) at most 12 rows name the same one
- gate_scores: bfloat16 [4096, 8], P('expert'), may hold values from 0.19921875 to 1
Outputs:
- mixed: bfloat16 [4096, 4096], P('expert', 'group')
Inputs may be any that keep to these rules, and one draw needn't show every extreme that they name: `expert_ids`: the 8 experts of a token are distinct; within the 64 rows of one device no expert is named by more than 12 rows, a bound that some block reaches.
All inputs are finite; a program needn't handle non-finite values.
Results may differ from a plain program's by a relative error of at most 0.019.
Values may be sent and summed in bfloat16 or wider, within the bound.
No kernel may reach another device: no remote copies, remote signals or barrier semaphores. Data moves between devices by JAX's collectives and lax.ppermute only.
A program may use at most 128 MiB of HBM per device.

v0:
```python
import jax
import jax.numpy as jnp
from jax import lax
from jax.sharding import PartitionSpec as P


def per_device(tokens, gate_weight, up_weight, down_weight, expert_ids, gate_scores):
    experts = lax.axis_size("expert")
    tok_rows = tokens.shape[0]
    top_count = expert_ids.shape[1]
    capacity = tok_rows * top_count * 3 // (2 * experts)
    flat_ids = expert_ids.reshape(-1)
    onehot = (flat_ids[:, None] == jnp.arange(experts, dtype=jnp.int32)[None, :]).astype(jnp.int32)
    before = jnp.cumsum(onehot, axis=0) - onehot
    slot_index = jnp.sum(before * onehot, axis=1).reshape(tok_rows, top_count)
    slot_keys = expert_ids * capacity + slot_index
    columns = jnp.arange(experts * capacity, dtype=jnp.int32)
    matches = slot_keys[:, :, None] == columns[None, None, :]
    selector = jnp.any(matches, axis=1).astype(jnp.bfloat16)
    weights = jnp.sum(
        jnp.where(matches, gate_scores[:, :, None].astype(jnp.float32), 0.0), axis=1
    ).astype(jnp.bfloat16)
    whole_rows = lax.all_gather(tokens, "group", axis=1, tiled=True)
    placed = lax.dot_general(
        selector, whole_rows, (((0,), (0,)), ((), ())), preferred_element_type=jnp.float32
    )
    arrived = lax.all_to_all(
        placed.astype(jnp.bfloat16).reshape(experts, capacity, whole_rows.shape[1]),
        "expert",
        split_axis=0,
        concat_axis=0,
        tiled=True,
    )
    row_block = arrived.reshape(-1, arrived.shape[2])
    gate_value = lax.dot_general(
        row_block, gate_weight[0], (((1,), (1,)), ((), ())), preferred_element_type=jnp.float32
    )
    up_value = lax.dot_general(
        row_block, up_weight[0], (((1,), (1,)), ((), ())), preferred_element_type=jnp.float32
    )
    hidden = (jax.nn.silu(gate_value) * up_value).astype(jnp.bfloat16)
    partial_value = jnp.dot(hidden, down_weight[0], preferred_element_type=jnp.float32)
    returned = lax.all_to_all(
        partial_value.astype(jnp.bfloat16).reshape(arrived.shape),
        "expert",
        split_axis=0,
        concat_axis=0,
        tiled=True,
    )
    combined = jnp.dot(
        weights, returned.reshape(experts * capacity, -1), preferred_element_type=jnp.float32
    )
    return lax.psum_scatter(combined.astype(jnp.bfloat16), "group", scatter_dimension=1, tiled=True)


def solution(mesh):
    placed = (
        P("expert", "group"),
        P("expert", "group", None),
        P("expert", "group", None),
        P("expert", "group", None),
        P("expert", None),
        P("expert", None),
    )
    return jax.shard_map(
        per_device, mesh=mesh, in_specs=placed, out_specs=P("expert", "group"), check_vma=False
    )
```

profile of v0, /device:TPU:1, one launch (start us, length us, event | category | flops | bytes accessed | tf_op | source)
XLA Modules:
  0.0 536.0 jit_solution(18164312794375199998)
XLA Ops:
  6.5 0.0 copy-start
  6.5 0.9 copy.21
  7.4 0.1 eq.42
  7.5 0.1 eq.38
  7.6 1.2 reduce-window.6
  8.8 0.2 slice_reduce_fusion
  9.1 0.1 fusion.22
  9.2 0.1 reshape.36
  9.3 0.1 copy.24
  9.4 0.7 multiply_add_fusion
  10.1 0.1 copy.25
  10.2 0.5 fusion.5
  10.7 22.0 %all_gather.3 = bf16[64,4096]{1,0:T(8,128)(2,1)S(1)} all-gather(bf16[64,512]{1,0:T(8,128)(2,1)} %param.6), channel_id=1, replica_groups=mesh['expert'=64,'group'=8] {'group'}, dimensions={1}, use_global_device_ids=true | all-gather | bytes 589824 | tf_op jit(solution)/shard_map/all_gather | solution.py:23
  32.7 4.6 convolution_convert_fusion
  37.3 9.8 %reshape.37 = bf16[64,12,4096]{2,1,0:T(8,128)(2,1)} reshape(bf16[768,4096]{1,0:T(8,128)(2,1)} %convolution_convert_fusion) | data formatting | bytes 12582912 | tf_op jit(solution)/shard_map/reshape | solution.py:28
  47.0 206.1 %all_to_all.10 = bf16[64,12,4096]{2,1,0:T(8,128)(2,1)} all-to-all(bf16[64,12,4096]{2,1,0:T(8,128)(2,1)} %reshape.37), channel_id=1, replica_groups=mesh['expert'=64,'group'=8] {'expert'}, dimensions={0} | all-to-all | bytes 12582912 | tf_op jit(solution)/shard_map/all_to_all | solution.py:27
  253.2 0.0 copy-start.2
  253.2 10.1 %reshape.38 = bf16[768,4096]{1,0:T(8,128)(2,1)} reshape(bf16[64,12,4096]{2,1,0:T(8,128)(2,1)} %all_to_all.10) | data formatting | bytes 12582912 | tf_op jit(solution)/shard_map/reshape | solution.py:34
  263.3 0.0 copy-done.2
  263.3 5.8 %fusion.3 = f32[768,192]{0,1:T(8,128)} fusion(bf16[768,4096]{1,0:T(8,128)(2,1)} %reshape.38, bf16[1,192,4096]{2,1,0:T(8,128)(2,1)S(1)} %copy-done.2), kind=kOutput, calls=%fused_computation.6 | convolution fusion | flops 1207959552 | bytes 8454144 | tf_op jit(solution)/shard_map/dot_general | solution.py:35
  269.1 0.0 copy-done
  269.1 13.5 %convolution_convert_fusion.1 = bf16[768,4096]{1,0:T(8,128)(2,1)} fusion(bf16[1,192,4096]{2,1,0:T(8,128)(2,1)S(1)} %copy-done, bf16[768,4096]{1,0:T(8,128)(2,1)} %reshape.38, bf16[1,192,4096]{2,1,0:T(8,128)(2,1)} %param.8, f32[768,192]{0,1:T(8,128)} %fusion.3), kind=kOutput, calls=%fused_computation.1 | convolution fusion | flops 2419949568 | bytes 16318464 | tf_op jit(solution)/shard_map/dot_general | solution.py:42
  282.6 9.8 %reshape.39 = bf16[64,12,4096]{2,1,0:T(8,128)(2,1)} reshape(bf16[768,4096]{1,0:T(8,128)(2,1)} %convolution_convert_fusion.1) | data formatting | bytes 12582912 | tf_op jit(solution)/shard_map/reshape | solution.py:44
  292.3 0.0 copy-start.1
  292.3 6.2 %all-to-all-start.1 = ((bf16[64,12,4096]{2,1,0:T(8,128)(2,1)}), bf16[64,12,4096]{2,1,0:T(8,128)(2,1)}, u32[]{:S(2)}, u32[]{:S(2)}) async-start(bf16[64,12,4096]{2,1,0:T(8,128)(2,1)} %reshape.39), calls=%async_computation.1 | async-start | bytes 16777216 | tf_op jit(solution)/shard_map/all_to_all | solution.py:43
  298.5 0.0 reduce-scatter.2.cloned.1.call-start
  298.5 0.0 copy-done.1
  298.6 0.1 copy.26
  298.7 0.6 select_reduce_fusion
  299.2 185.0 %all-to-all-done.1 = bf16[64,12,4096]{2,1,0:T(8,128)(2,1)} async-done(((bf16[64,12,4096]{2,1,0:T(8,128)(2,1)}), bf16[64,12,4096]{2,1,0:T(8,128)(2,1)}, u32[]{:S(2)}, u32[]{:S(2)}) %all-to-all-start.1) | async-done | bytes 6291488 | tf_op jit(solution)/shard_map/all_to_all | solution.py:43
  484.2 9.9 %reshape.40 = bf16[768,4096]{1,0:T(8,128)(2,1)} reshape(bf16[64,12,4096]{2,1,0:T(8,128)(2,1)} %all-to-all-done.1) | data formatting | bytes 12582912 | tf_op jit(solution)/shard_map/reshape | solution.py:51
  494.1 4.8 convolution_convert_fusion.2
  498.9 0.0 reduce-scatter.2.cloned.1.call-update
  498.9 30.2 %reduce-scatter.2.cloned.1.call-done = bf16[64,512]{1,0:T(8,128)(2,1)} async-done(((bf16[64,4096]{1,0:T(8,128)(2,1)}), bf16[64,512]{1,0:T(8,128)(2,1)}) %reduce-scatter.2.cloned.1.call-update) | async-done | bytes 65552 | tf_op jit(solution)/shard_map/reduce_scatter | solution.py:53
  (3 shorter events, 0.1 us)
Async XLA Ops:
  6.5 262.6 %copy-start = (bf16[1,192,4096]{2,1,0:T(8,128)(2,1)S(1)}, bf16[1,192,4096]{2,1,0:T(8,128)(2,1)}, u32[]{:S(2)}) copy-start(bf16[1,192,4096]{2,1,0:T(8,128)(2,1)} %param.9) | copy-start | bytes 4718596
  253.2 10.1 %copy-start.2 = (bf16[1,192,4096]{2,1,0:T(8,128)(2,1)S(1)}, bf16[1,192,4096]{2,1,0:T(8,128)(2,1)}, u32[]{:S(2)}) copy-start(bf16[1,192,4096]{2,1,0:T(8,128)(2,1)} %param.7) | copy-start | bytes 4718596
  292.3 6.2 %copy-start.1 = (bf16[64,8]{0,1:T(8,128)(2,1)S(1)}, bf16[64,8]{0,1:T(8,128)(2,1)}, u32[]{:S(2)}) copy-start(bf16[64,8]{0,1:T(8,128)(2,1)} %param.11) | copy-start | bytes 3076
  292.3 191.9 %all-to-all-start.1 = ((bf16[64,12,4096]{2,1,0:T(8,128)(2,1)}), bf16[64,12,4096]{2,1,0:T(8,128)(2,1)}, u32[]{:S(2)}, u32[]{:S(2)}) async-start(bf16[64,12,4096]{2,1,0:T(8,128)(2,1)} %reshape.39), calls=%async_computation.1 | async-start | bytes 16777216 | tf_op jit(solution)/shard_map/all_to_all | solution.py:43
  298.5 230.6 %reduce-scatter.2.cloned.1.call-start = ((), (), s32[]{:S(2)}) async-start(), calls=%async_computation.3 | async-start | bytes 589824 | tf_op jit(solution)/shard_map/reduce_scatter | solution.py:53
Sparse Core Ops, SparseCore 0:
  499.0 30.0 reduce-scatter.1
where the time goes:
time: 541 us; the launch traced here: 536 us
  blocking collectives  228 us (42%)
  waiting for transfers between devices  215 us (40%)
  local copies, waits for them, and re-layouts  41.1 us (8%)
  matrix products  28.6 us (5%)
  between operations  13.5 us (2%)
  starting transfers between devices  6.19 us (1%)
    all_to_all x1, blocking collectives, per_device(): lax.all_to_all(placed.astype(jnp.bfloat16).reshape(experts, capacity, who...  206 us
    all_to_all x1, waiting for transfers between devices, per_device(): lax.all_to_all(partial_value.astype(jnp.bfloat16).reshape(arrived.shape),...  185 us
    reduce_scatter x1, waiting for transfers between devices, per_device(): lax.psum_scatter(combined.astype(jnp.bfloat16), 'group', scatter_dimensio...  30.2 us
    all_gather x1, blocking collectives, per_device(): whole_rows = lax.all_gather(tokens, 'group', axis=1, tiled=True)  22 us
    dot_general x1, matrix products, per_device(): jnp.dot(hidden, down_weight[0], preferred_element_type=jnp.float32)  13.5 us
  transfers between devices with their start and end apart: 2, of which 2 were waited for; matrix products, arithmetic and copies ran while one was open for 0% of the time, Pallas kernels for 0%

commit v1 on v0

v1 whole, which is shorter than its diff:
```python
import jax
import jax.numpy as jnp
from jax import lax
from jax.sharding import PartitionSpec as P


def route_tables(expert_ids, gate_scores, experts):
    tok_rows, top_count = expert_ids.shape
    capacity = tok_rows * top_count * 3 // (2 * experts)
    flat_ids = expert_ids.reshape(-1)
    onehot = (flat_ids[:, None] == jnp.arange(experts, dtype=jnp.int32)[None, :]).astype(jnp.int32)
    before = jnp.cumsum(onehot, axis=0) - onehot
    slot_index = jnp.sum(before * onehot, axis=1).reshape(tok_rows, top_count)
    slot_keys = expert_ids * capacity + slot_index
    columns = jnp.arange(experts * capacity, dtype=jnp.int32)
    matches = slot_keys[:, :, None] == columns[None, None, :]
    selector = jnp.any(matches, axis=1).astype(jnp.bfloat16)
    weights = jnp.sum(
        jnp.where(matches, gate_scores[:, :, None].astype(jnp.float32), 0.0), axis=1
    ).astype(jnp.bfloat16)
    return capacity, selector, weights


def per_device(tokens, gate_weight, up_weight, down_weight, expert_ids, gate_scores):
    experts = lax.axis_size("expert")
    capacity, selector, weights = route_tables(expert_ids, gate_scores, experts)
    placed = lax.dot_general(
        selector, tokens, (((0,), (0,)), ((), ())), preferred_element_type=jnp.float32
    ).astype(jnp.bfloat16)
    arrived = lax.all_to_all(
        placed.reshape(experts, capacity, tokens.shape[1]), "expert", 0, 0, tiled=True
    ).reshape(experts * capacity, tokens.shape[1])
    row_block = lax.all_gather(arrived, "group", axis=1, tiled=True)
    gate_value = lax.dot_general(
        row_block, gate_weight[0], (((1,), (1,)), ((), ())), preferred_element_type=jnp.float32
    )
    up_value = lax.dot_general(
        row_block, up_weight[0], (((1,), (1,)), ((), ())), preferred_element_type=jnp.float32
    )
    hidden = (jax.nn.silu(gate_value) * up_value).astype(jnp.bfloat16)
    partial_value = jnp.dot(hidden, down_weight[0], preferred_element_type=jnp.float32)
    summed = lax.psum_scatter(
        partial_value.astype(jnp.bfloat16), "group", scatter_dimension=1, tiled=True
    )
    returned = lax.all_to_all(
        summed.reshape(experts, capacity, summed.shape[1]), "expert", 0, 0, tiled=True
    ).reshape(experts * capacity, summed.shape[1])
    combined = jnp.dot(weights, returned, preferred_element_type=jnp.float32)
    return combined.astype(jnp.bfloat16)


def solution(mesh):
    placed = (
        P("expert", "group"),
        P("expert", "group", None),
        P("expert", "group", None),
        P("expert", "group", None),
        P("expert", None),
        P("expert", None),
    )
    return jax.shard_map(
        per_device, mesh=mesh, in_specs=placed, out_specs=P("expert", "group"), check_vma=False
    )
```

time: 541 us -> 277 us (0.51)
  blocking collectives: 228 us -> 43.3 us
  waiting for transfers between devices: 215 us -> 178 us
  local copies, waits for them, and re-layouts: 41.1 us -> 6.31 us
  matrix products: 28.6 us -> 21.4 us
    all_to_all x1, blocking collectives: 206 us -> 43.3 us  [per_device(): lax.all_to_all(placed.reshape(experts, capacity, tokens.shape[1]), 'exper...]
    all_to_all x1, waiting for transfers between devices: 185 us -> 27.9 us  [per_device(): lax.all_to_all(summed.reshape(experts, capacity, summed.shape[1]), 'exper...]
    all_gather x0 -> x1, waiting for transfers between devices: none -> 73.5 us  [per_device(): row_block = lax.all_gather(arrived, 'group', axis=1, tiled=True)]
    reduce_scatter x1, waiting for transfers between devices: 30.2 us -> 76.7 us  [per_device(): lax.psum_scatter(partial_value.astype(jnp.bfloat16), 'group', scatter_dim...]
    reshape x6, local copies, waits for them, and re-layouts: 39.6 us -> 4.81 us  [the longest x1 2.2 us: per_device(): arrived = lax.all_to_all(placed.reshape(experts, capacity, tokens.shape[1...]
    all_gather x1 -> x0, blocking collectives: 22 us -> none  [per_device(): whole_rows = lax.all_gather(tokens, 'group', axis=1, tiled=True)]
    dot_general x2, matrix products: 9.34 us -> 2.15 us  [the longest x1 1.26 us: per_device(): lax.dot_general(selector, tokens, (((0,), (0,)), ((), ())), preferred_ele...]
  transfers between devices with their start and end apart: 2 -> 3, of which waited for: 2 -> 3; matrix products, arithmetic and copies ran while one was open for 0% -> 0% of each run, Pallas kernels for 0% -> 0%
where the time goes in v1:
time: 277 us
  waiting for transfers between devices  178 us (64%)
  blocking collectives  43.3 us (16%)
  matrix products  21.4 us (8%)
  between operations  13.5 us (5%)
  starting transfers between devices  11.1 us (4%)
  local copies, waits for them, and re-layouts  6.31 us (2%)
  other arithmetic  3.18 us (1%)
    reduce_scatter x1, waiting for transfers between devices, per_device(): lax.psum_scatter(partial_value.astype(jnp.bfloat16), 'group', scatter_dim...  76.7 us
    all_gather x1, waiting for transfers between devices, per_device(): row_block = lax.all_gather(arrived, 'group', axis=1, tiled=True)  73.5 us
    all_to_all x1, blocking collectives, per_device(): lax.all_to_all(placed.reshape(experts, capacity, tokens.shape[1]), 'exper...  43.3 us
    all_to_all x1, waiting for transfers between devices, per_device(): lax.all_to_all(summed.reshape(experts, capacity, summed.shape[1]), 'exper...  27.9 us
    dot_general x1, matrix products, per_device(): jnp.dot(hidden, down_weight[0], preferred_element_type=jnp.float32)  13.5 us
    all_to_all x1, starting transfers between devices, per_device(): lax.all_to_all(summed.reshape(experts, capacity, summed.shape[1]), 'exper...  11.1 us
    dot_general x1, matrix products, per_device(): lax.dot_general(row_block, gate_weight[0], (((1,), (1,)), ((), ())), pref...  5.85 us
  transfers between devices with their start and end apart: 3, of which 3 were waited for; matrix products, arithmetic and copies ran while one was open for 0% of the time, Pallas kernels for 0%

profile of v1, /device:TPU:1, one launch (start us, length us, event | category | flops | bytes accessed | tf_op | source)
XLA Modules:
  0.0 276.9 jit_solution(11767878892583702980)
XLA Ops:
  6.5 0.0 copy-start
  6.5 0.0 all-gather.2.cloned.1.call-start
  6.5 0.9 copy.21
  7.4 0.1 eq.42
  7.5 0.1 eq.38
  7.6 1.2 reduce-window.6
  8.8 0.2 slice_reduce_fusion
  9.1 0.1 fusion.22
  9.2 0.1 reshape.36
  9.3 0.1 copy.24
  9.4 0.7 multiply_add_fusion
  10.1 0.1 copy.25
  10.2 0.5 fusion.5
  10.7 1.3 convolution_convert_fusion.1
  12.0 0.2 reshape.37
  12.2 43.3 %all_to_all.10 = bf16[64,12,512]{2,1,0:T(8,128)(2,1)} all-to-all(bf16[64,12,512]{2,1,0:T(8,128)(2,1)S(1)} %reshape.37), channel_id=1, replica_groups=mesh['expert'=64,'group'=8] {'expert'}, dimensions={0} | all-to-all | bytes 1572864 | tf_op jit(solution)/shard_map/all_to_all | solution.py:30
  55.4 0.0 copy-start.2
  55.4 2.2 reshape.38
  57.6 0.0 all-gather.2.cloned.1.call-update
  57.7 0.0 reduce-scatter.2.cloned.1.call-start
  57.7 73.5 %all-gather.2.cloned.1.call-done = bf16[768,4096]{1,0:T(8,128)(2,1)} async-done(((bf16[768,512]{1,0:T(8,128)(2,1)}), bf16[768,4096]{1,0:T(8,128)(2,1)}) %all-gather.2.cloned.1.call-update) | async-done | bytes 6291472 | tf_op jit(solution)/shard_map/all_gather | solution.py:33
  131.2 0.0 copy-done.2
  131.2 5.8 %fusion.3 = f32[768,192]{0,1:T(8,128)} fusion(bf16[768,4096]{1,0:T(8,128)(2,1)} %all-gather.2.cloned.1.call-done, bf16[1,192,4096]{2,1,0:T(8,128)(2,1)S(1)} %copy-done.2), kind=kOutput, calls=%fused_computation.4 | convolution fusion | flops 1207959552 | bytes 8454144 | tf_op jit(solution)/shard_map/dot_general | solution.py:34
  137.1 0.0 copy-done
  137.1 13.5 %convolution_convert_fusion = bf16[768,4096]{1,0:T(8,128)(2,1)} fusion(bf16[1,192,4096]{2,1,0:T(8,128)(2,1)S(1)} %copy-done, bf16[768,4096]{1,0:T(8,128)(2,1)} %all-gather.2.cloned.1.call-done, bf16[1,192,4096]{2,1,0:T(8,128)(2,1)} %param.8, f32[768,192]{0,1:T(8,128)} %fusion.3), kind=kOutput, calls=%fused_computation | convolution fusion | flops 2419949568 | bytes 16318464 | tf_op jit(solution)/shard_map/dot_general | solution.py:41
  150.5 0.0 reduce-scatter.2.cloned.1.call-update
  150.6 0.0 copy-start.1
  150.6 76.7 %reduce-scatter.2.cloned.1.call-done = bf16[768,512]{1,0:T(8,128)(2,1)} async-done(((bf16[768,4096]{1,0:T(8,128)(2,1)}), bf16[768,512]{1,0:T(8,128)(2,1)}) %reduce-scatter.2.cloned.1.call-update) | async-done | bytes 786448 | tf_op jit(solution)/shard_map/reduce_scatter | solution.py:42
  227.3 2.1 reshape.39
  229.4 11.1 %all-to-all-start.1 = ((bf16[64,12,512]{2,1,0:T(8,128)(2,1)}), bf16[64,12,512]{2,1,0:T(8,128)(2,1)S(1)}, u32[]{:S(2)}, u32[]{:S(2)}) async-start(bf16[64,12,512]{2,1,0:T(8,128)(2,1)} %reshape.39), calls=%async_computation.2 | async-start | bytes 2097152 | tf_op jit(solution)/shard_map/all_to_all | solution.py:45
  240.5 0.0 copy-done.1
  240.5 0.1 copy.26
  240.6 0.6 select_reduce_fusion
  241.2 27.9 %all-to-all-done.1 = bf16[64,12,512]{2,1,0:T(8,128)(2,1)S(1)} async-done(((bf16[64,12,512]{2,1,0:T(8,128)(2,1)}), bf16[64,12,512]{2,1,0:T(8,128)(2,1)S(1)}, u32[]{:S(2)}, u32[]{:S(2)}) %all-to-all-start.1) | async-done | bytes 786464 | tf_op jit(solution)/shard_map/all_to_all | solution.py:45
  269.0 0.2 reshape.40
  269.2 0.9 convolution_convert_fusion.2
  (3 shorter events, 0.1 us)
Async XLA Ops:
  6.5 130.5 %copy-start = (bf16[1,192,4096]{2,1,0:T(8,128)(2,1)S(1)}, bf16[1,192,4096]{2,1,0:T(8,128)(2,1)}, u32[]{:S(2)}) copy-start(bf16[1,192,4096]{2,1,0:T(8,128)(2,1)} %param.9) | copy-start | bytes 4718596
  6.5 124.7 %all-gather.2.cloned.1.call-start = ((), (), s32[]{:S(2)}) async-start(), calls=%async_computation.3 | async-start | bytes 7077888 | tf_op jit(solution)/shard_map/all_gather | solution.py:33
  55.4 75.8 %copy-start.2 = (bf16[1,192,4096]{2,1,0:T(8,128)(2,1)S(1)}, bf16[1,192,4096]{2,1,0:T(8,128)(2,1)}, u32[]{:S(2)}) copy-start(bf16[1,192,4096]{2,1,0:T(8,128)(2,1)} %param.7) | copy-start | bytes 4718596
  57.7 169.6 %reduce-scatter.2.cloned.1.call-start = ((), (), s32[]{:S(2)}) async-start(), calls=%async_computation.4 | async-start | bytes 7077888 | tf_op jit(solution)/shard_map/reduce_scatter | solution.py:42
  150.6 89.9 %copy-start.1 = (bf16[64,8]{0,1:T(8,128)(2,1)S(1)}, bf16[64,8]{0,1:T(8,128)(2,1)}, u32[]{:S(2)}) copy-start(bf16[64,8]{0,1:T(8,128)(2,1)} %param.11) | copy-start | bytes 3076
  229.4 39.6 %all-to-all-start.1 = ((bf16[64,12,512]{2,1,0:T(8,128)(2,1)}), bf16[64,12,512]{2,1,0:T(8,128)(2,1)S(1)}, u32[]{:S(2)}, u32[]{:S(2)}) async-start(bf16[64,12,512]{2,1,0:T(8,128)(2,1)} %reshape.39), calls=%async_computation.2 | async-start | bytes 2097152 | tf_op jit(solution)/shard_map/all_to_all | solution.py:45
Sparse Core Ops, SparseCore 0:
  57.8 73.4 all-gather.1
  150.7 76.5 reduce-scatter.1

commit v2 on v1

--- a/solution.py
+++ b/solution.py
@@ -2,6 +2,8 @@
 import jax.numpy as jnp
 from jax import lax
 from jax.sharding import PartitionSpec as P
+
+CHUNKS = 2
 
 
 def route_tables(expert_ids, gate_scores, experts):
@@ -21,15 +23,10 @@
     return capacity, selector, weights
 
 
-def per_device(tokens, gate_weight, up_weight, down_weight, expert_ids, gate_scores):
-    experts = lax.axis_size("expert")
-    capacity, selector, weights = route_tables(expert_ids, gate_scores, experts)
-    placed = lax.dot_general(
-        selector, tokens, (((0,), (0,)), ((), ())), preferred_element_type=jnp.float32
-    ).astype(jnp.bfloat16)
+def expert_rows(chunk, gate_weight, up_weight, down_weight, experts, width):
     arrived = lax.all_to_all(
-        placed.reshape(experts, capacity, tokens.shape[1]), "expert", 0, 0, tiled=True
-    ).reshape(experts * capacity, tokens.shape[1])
+        chunk.reshape(experts, -1, width), "expert", 0, 0, tiled=True
+    ).reshape(-1, width)
     row_block = lax.all_gather(arrived, "group", axis=1, tiled=True)
     gate_value = lax.dot_general(
         row_block, gate_weight[0], (((1,), (1,)), ((), ())), preferred_element_type=jnp.float32
@@ -42,9 +39,24 @@
     summed = lax.psum_scatter(
         partial_value.astype(jnp.bfloat16), "group", scatter_dimension=1, tiled=True
     )
-    returned = lax.all_to_all(
-        summed.reshape(experts, capacity, summed.shape[1]), "expert", 0, 0, tiled=True
-    ).reshape(experts * capacity, summed.shape[1])
+    return lax.all_to_all(
+        summed.reshape(experts, -1, width), "expert", 0, 0, tiled=True
+    )
+
+
+def per_device(tokens, gate_weight, up_weight, down_weight, expert_ids, gate_scores):
+    experts = lax.axis_size("expert")
+    width = tokens.shape[1]
+    capacity, selector, weights = route_tables(expert_ids, gate_scores, experts)
+    placed = lax.dot_general(
+        selector, tokens, (((0,), (0,)), ((), ())), preferred_element_type=jnp.float32
+    ).astype(jnp.bfloat16).reshape(experts, capacity, width)
+    cut = capacity // CHUNKS
+    pieces = []
+    for c in range(CHUNKS):
+        chunk = placed[:, c * cut:(c + 1) * cut]
+        pieces.append(expert_rows(chunk, gate_weight, up_weight, down_weight, experts, width))
+    returned = jnp.concatenate(pieces, axis=1).reshape(experts * capacity, width)
     combined = jnp.dot(weights, returned, preferred_element_type=jnp.float32)
     return combined.astype(jnp.bfloat16)
 

time: 277 us -> 281 us (1.014)
  waiting for transfers between devices: 178 us -> 150 us
  starting transfers between devices: 11.1 us -> 28.8 us
  blocking collectives: 43.3 us -> 55.3 us
    all_to_all x1 -> x2, starting transfers between devices: 11.1 us -> 28.7 us  [expert_rows(): lax.all_to_all(summed.reshape(experts, -1, width), 'expert', 0, 0, tiled=...]
    all_gather x1 -> x2, waiting for transfers between devices: 73.5 us -> 58.1 us  [expert_rows(): row_block = lax.all_gather(arrived, 'group', axis=1, tiled=True)]
    all_to_all x1 -> x2, blocking collectives: 43.3 us -> 55.3 us  [expert_rows(): lax.all_to_all(chunk.reshape(experts, -1, width), 'expert', 0, 0, tiled=T...]
    all_to_all x1 -> x2, waiting for transfers between devices: 27.9 us -> 16.5 us  [expert_rows(): lax.all_to_all(summed.reshape(experts, -1, width), 'expert', 0, 0, tiled=...]
    reduce_scatter x1 -> x2, waiting for transfers between devices: 76.7 us -> 74.9 us  [expert_rows(): lax.psum_scatter(partial_value.astype(jnp.bfloat16), 'group', scatter_dim...]
    reshape x4 -> x6, local copies, waits for them, and re-layouts: 4.67 us -> 5.97 us  [the longest x2 3.85 us: expert_rows(): summed.reshape(experts, -1, width)]
    dot_general x2 -> x4, matrix products: 19.3 us -> 19.1 us  [the longest x2 12.1 us: expert_rows(): jnp.dot(hidden, down_weight[0], preferred_element_type=jnp.float32)]
  transfers between devices with their start and end apart: 3 -> 6, of which waited for: 3 -> 5; matrix products, arithmetic and copies ran while one was open for 0% -> 9% of each run, Pallas kernels for 0% -> 0%
where the time goes in v2:
time: 281 us
  waiting for transfers between devices  150 us (53%)
  blocking collectives  55.3 us (20%)
  starting transfers between devices  28.8 us (10%)
  matrix products  21.3 us (8%)
  between operations  13.3 us (5%)
  local copies, waits for them, and re-layouts  7.79 us (3%)
  other arithmetic  4.58 us (2%)
    reduce_scatter x2, waiting for transfers between devices, expert_rows(): lax.psum_scatter(partial_value.astype(jnp.bfloat16), 'group', scatter_dim...  74.9 us
    all_gather x2, waiting for transfers between devices, expert_rows(): row_block = lax.all_gather(arrived, 'group', axis=1, tiled=True)  58.1 us
    all_to_all x2, blocking collectives, expert_rows(): lax.all_to_all(chunk.reshape(experts, -1, width), 'expert', 0, 0, tiled=T...  55.3 us
    all_to_all x2, starting transfers between devices, expert_rows(): lax.all_to_all(summed.reshape(experts, -1, width), 'expert', 0, 0, tiled=...  28.7 us
    all_to_all x2, waiting for transfers between devices, expert_rows(): lax.all_to_all(summed.reshape(experts, -1, width), 'expert', 0, 0, tiled=...  16.5 us
    dot_general x2, matrix products, expert_rows(): jnp.dot(hidden, down_weight[0], preferred_element_type=jnp.float32)  12.1 us
    dot_general x2, matrix products, expert_rows(): lax.dot_general(row_block, gate_weight[0], (((1,), (1,)), ((), ())), pref...  7.06 us
  transfers between devices with their start and end apart: 6, of which 5 were waited for; matrix products, arithmetic and copies ran while one was open for 9% of the time, Pallas kernels for 0%

profile of v2, /device:TPU:1, one launch (start us, length us, event | category | flops | bytes accessed | tf_op | source)
XLA Modules:
  0.0 280.7 jit_solution(13622737630275665636)
XLA Ops:
  6.5 0.0 copy-start
  6.5 0.0 all-gather.3.cloned.1.call-start
  6.5 0.9 copy.21
  7.4 0.1 eq.42
  7.5 0.1 eq.38
  7.6 1.2 reduce-window.6
  8.8 0.2 slice_reduce_fusion
  9.1 0.1 fusion.41
  9.2 0.1 reshape.42
  9.3 0.1 copy.24
  9.4 0.7 multiply_add_fusion
  10.1 0.1 copy.25
  10.2 0.5 fusion.10
  10.7 1.3 convolution_convert_fusion.2
  12.0 0.2 reshape.43
  12.2 0.2 fusion.46
  12.4 31.9 %all_to_all.20 = bf16[64,6,512]{2,1,0:T(8,128)(2,1)S(1)} all-to-all(bf16[64,6,512]{2,1,0:T(8,128)(2,1)S(1)} %get-tuple-element.5), channel_id=1, replica_groups=mesh['expert'=64,'group'=8] {'expert'}, dimensions={0} | all-to-all | bytes 786432 | tf_op jit(solution)/shard_map/all_to_all | solution.py:27
  44.3 0.9 reshape.44
  45.1 0.0 all-gather.3.cloned.1.call-update
  45.2 0.0 all-gather.5.cloned.1.call-start
  45.2 23.4 %all_to_all.21 = bf16[64,6,512]{2,1,0:T(8,128)(2,1)S(1)} all-to-all(bf16[64,6,512]{2,1,0:T(8,128)(2,1)S(1)} %get-tuple-element.6), channel_id=1, replica_groups=mesh['expert'=64,'group'=8] {'expert'}, dimensions={0} | all-to-all | bytes 786432 | tf_op jit(solution)/shard_map/all_to_all | solution.py:27
  68.6 0.9 reshape.46
  69.5 0.0 all-gather.5.cloned.1.call-update
  69.5 0.0 copy-start.1
  69.5 0.0 reduce-scatter.3.cloned.1.call-start
  69.6 19.2 %all-gather.3.cloned.1.call-done = bf16[384,4096]{1,0:T(8,128)(2,1)} async-done(((bf16[384,512]{1,0:T(8,128)(2,1)}), bf16[384,4096]{1,0:T(8,128)(2,1)}) %all-gather.3.cloned.1.call-update) | async-done | bytes 3145744 | tf_op jit(solution)/shard_map/all_gather | solution.py:30
  88.8 3.5 %fusion.8 = f32[384,192]{0,1:T(8,128)S(1)} fusion(bf16[384,4096]{1,0:T(8,128)(2,1)} %all-gather.3.cloned.1.call-done, bf16[1,192,4096]{2,1,0:T(8,128)(2,1)} %param.7), kind=kOutput, calls=%fused_computation.10 | convolution fusion | flops 603979776 | bytes 5013504 | tf_op jit(solution)/shard_map/dot_general | solution.py:31
  92.4 0.0 copy-done
  92.4 0.0 copy-done.1
  92.4 6.0 %convolution_convert_fusion.1 = bf16[384,4096]{1,0:T(8,128)(2,1)} fusion(bf16[1,192,4096]{2,1,0:T(8,128)(2,1)S(1)} %copy-done, bf16[384,4096]{1,0:T(8,128)(2,1)} %all-gather.3.cloned.1.call-done, bf16[1,192,4096]{2,1,0:T(8,128)(2,1)S(1)} %copy-done.1, f32[384,192]{0,1:T(8,128)S(1)} %fusion.8), kind=kOutput, calls=%fused_computation.1 | convolution fusion | flops 1209974784 | bytes 9732096 | tf_op jit(solution)/shard_map/dot_general | solution.py:38
  98.4 0.0 reduce-scatter.3.cloned.1.call-update
  98.4 0.0 reduce-scatter.5.cloned.1.call-start
  98.5 38.9 %all-gather.5.cloned.1.call-done = bf16[384,4096]{1,0:T(8,128)(2,1)} async-done(((bf16[384,512]{1,0:T(8,128)(2,1)}), bf16[384,4096]{1,0:T(8,128)(2,1)}) %all-gather.5.cloned.1.call-update) | async-done | bytes 3145744 | tf_op jit(solution)/shard_map/all_gather | solution.py:30
  137.4 3.5 %fusion.6 = f32[384,192]{0,1:T(8,128)S(1)} fusion(bf16[384,4096]{1,0:T(8,128)(2,1)} %all-gather.5.cloned.1.call-done, bf16[1,192,4096]{2,1,0:T(8,128)(2,1)} %param.7), kind=kOutput, calls=%fused_computation.8 | convolution fusion | flops 603979776 | bytes 5013504 | tf_op jit(solution)/shard_map/dot_general | solution.py:31
  140.9 6.0 %convolution_convert_fusion = bf16[384,4096]{1,0:T(8,128)(2,1)} fusion(bf16[1,192,4096]{2,1,0:T(8,128)(2,1)S(1)} %copy-done, bf16[384,4096]{1,0:T(8,128)(2,1)} %all-gather.5.cloned.1.call-done, bf16[1,192,4096]{2,1,0:T(8,128)(2,1)S(1)} %copy-done.1, f32[384,192]{0,1:T(8,128)S(1)} %fusion.6), kind=kOutput, calls=%fused_computation | convolution fusion | flops 1209974784 | bytes 9732096 | tf_op jit(solution)/shard_map/dot_general | solution.py:38
  146.9 0.0 reduce-scatter.5.cloned.1.call-update
  147.0 39.2 %reduce-scatter.3.cloned.1.call-done = bf16[384,512]{1,0:T(8,128)(2,1)} async-done(((bf16[384,4096]{1,0:T(8,128)(2,1)}), bf16[384,512]{1,0:T(8,128)(2,1)}) %reduce-scatter.3.cloned.1.call-update) | async-done | bytes 393232 | tf_op jit(solution)/shard_map/reduce_scatter | solution.py:39
  186.1 1.9 reshape.45
  188.0 0.0 copy-start.2
  188.0 14.4 %all-to-all-start.1 = ((bf16[64,6,512]{2,1,0:T(8,128)(2,1)}), bf16[64,6,512]{2,1,0:T(8,128)(2,1)S(1)}, u32[]{:S(2)}, u32[]{:S(2)}) async-start(bf16[64,6,512]{2,1,0:T(8,128)(2,1)} %reshape.45), calls=%async_computation.2 | async-start | bytes 1048576 | tf_op jit(solution)/shard_map/all_to_all | solution.py:42
  202.4 35.8 %reduce-scatter.5.cloned.1.call-done = bf16[384,512]{1,0:T(8,128)(2,1)} async-done(((bf16[384,4096]{1,0:T(8,128)(2,1)}), bf16[384,512]{1,0:T(8,128)(2,1)}) %reduce-scatter.5.cloned.1.call-update) | async-done | bytes 393232 | tf_op jit(solution)/shard_map/reduce_scatter | solution.py:39
  238.2 1.9 reshape.47
  240.1 0.0 all-to-all-done.1
  240.1 14.4 %all-to-all-start.3 = ((bf16[64,6,512]{2,1,0:T(8,128)(2,1)}), bf16[64,6,512]{2,1,0:T(8,128)(2,1)}, u32[]{:S(2)}, u32[]{:S(2)}) async-start(bf16[64,6,512]{2,1,0:T(8,128)(2,1)} %reshape.47), calls=%async_computation.5 | async-start | bytes 1048576 | tf_op jit(solution)/shard_map/all_to_all | solution.py:42
  254.5 0.0 copy-done.2
  254.5 0.1 copy.26
  254.6 0.6 select_reduce_fusion
  255.2 16.5 %all-to-all-done.3 = bf16[64,6,512]{2,1,0:T(8,128)(2,1)} async-done(((bf16[64,6,512]{2,1,0:T(8,128)(2,1)}), bf16[64,6,512]{2,1,0:T(8,128)(2,1)}, u32[]{:S(2)}, u32[]{:S(2)}) %all-to-all-start.3) | async-done | bytes 393248 | tf_op jit(solution)/shard_map/all_to_all | solution.py:42
  271.7 1.4 pad_maximum_fusion
  273.1 0.2 reshape.48
  273.3 0.9 convolution_convert_fusion.3
  (3 shorter events, 0.1 us)
Async XLA Ops:
  6.5 85.8 %copy-start = (bf16[1,192,4096]{2,1,0:T(8,128)(2,1)S(1)}, bf16[1,192,4096]{2,1,0:T(8,128)(2,1)}, u32[]{:S(2)}) copy-start(bf16[1,192,4096]{2,1,0:T(8,128)(2,1)} %param.9) | copy-start | bytes 4718596
  6.5 82.3 %all-gather.3.cloned.1.call-start = ((), (), s32[]{:S(2)}) async-start(), calls=%async_computation.6 | async-start | bytes 3538944 | tf_op jit(solution)/shard_map/all_gather | solution.py:30
  45.2 92.2 %all-gather.5.cloned.1.call-start = ((), (), s32[]{:S(2)}) async-start(), calls=%async_computation.8 | async-start | bytes 3538944 | tf_op jit(solution)/shard_map/all_gather | solution.py:30
  69.5 22.8 %copy-start.1 = (bf16[1,192,4096]{2,1,0:T(8,128)(2,1)S(1)}, bf16[1,192,4096]{2,1,0:T(8,128)(2,1)}, u32[]{:S(2)}) copy-start(bf16[1,192,4096]{2,1,0:T(8,128)(2,1)} %param.8) | copy-start | bytes 4718596
  69.5 116.6 %reduce-scatter.3.cloned.1.call-start = ((), (), s32[]{:S(2)}) async-start(), calls=%async_computation.7 | async-start | bytes 3538944 | tf_op jit(solution)/shard_map/reduce_scatter | solution.py:39
  98.4 139.8 %reduce-scatter.5.cloned.1.call-start = ((), (), s32[]{:S(2)}) async-start(), calls=%async_computation.9 | async-start | bytes 3538944 | tf_op jit(solution)/shard_map/reduce_scatter | solution.py:39
  188.0 66.5 %copy-start.2 = (bf16[64,8]{0,1:T(8,128)(2,1)S(1)}, bf16[64,8]{0,1:T(8,128)(2,1)}, u32[]{:S(2)}) copy-start(bf16[64,8]{0,1:T(8,128)(2,1)} %param.11) | copy-start | bytes 3076
  188.0 52.1 %all-to-all-start.1 = ((bf16[64,6,512]{2,1,0:T(8,128)(2,1)}), bf16[64,6,512]{2,1,0:T(8,128)(2,1)S(1)}, u32[]{:S(2)}, u32[]{:S(2)}) async-start(bf16[64,6,512]{2,1,0:T(8,128)(2,1)} %reshape.45), calls=%async_computation.2 | async-start | bytes 1048576 | tf_op jit(solution)/shard_map/all_to_all | solution.py:42
  240.1 31.6 %all-to-all-start.3 = ((bf16[64,6,512]{2,1,0:T(8,128)(2,1)}), bf16[64,6,512]{2,1,0:T(8,128)(2,1)}, u32[]{:S(2)}, u32[]{:S(2)}) async-start(bf16[64,6,512]{2,1,0:T(8,128)(2,1)} %reshape.47), calls=%async_computation.5 | async-start | bytes 1048576 | tf_op jit(solution)/shard_map/all_to_all | solution.py:42
Sparse Core Ops, SparseCore 0:
  45.3 43.4 all-gather.2
  90.9 46.4 all-gather.4
  140.2 45.8 reduce-scatter.2
  188.8 49.3 reduce-scatter.4

commit v3 on v1

--- a/solution.py
+++ b/solution.py
@@ -38,13 +38,12 @@
         row_block, up_weight[0], (((1,), (1,)), ((), ())), preferred_element_type=jnp.float32
     )
     hidden = (jax.nn.silu(gate_value) * up_value).astype(jnp.bfloat16)
-    partial_value = jnp.dot(hidden, down_weight[0], preferred_element_type=jnp.float32)
-    summed = lax.psum_scatter(
-        partial_value.astype(jnp.bfloat16), "group", scatter_dimension=1, tiled=True
-    )
+    hidden_all = lax.all_gather(hidden, "group", axis=1, tiled=True)
+    down_cols = lax.all_to_all(down_weight[0], "group", 1, 0, tiled=True)
+    partial_value = jnp.dot(hidden_all, down_cols, preferred_element_type=jnp.float32)
     returned = lax.all_to_all(
-        summed.reshape(experts, capacity, summed.shape[1]), "expert", 0, 0, tiled=True
-    ).reshape(experts * capacity, summed.shape[1])
+        partial_value.astype(jnp.bfloat16).reshape(experts, capacity, -1), "expert", 0, 0, tiled=True
+    ).reshape(experts * capacity, -1)
     combined = jnp.dot(weights, returned, preferred_element_type=jnp.float32)
     return combined.astype(jnp.bfloat16)
 

time: 277 us -> 262 us (0.946)
  waiting for transfers between devices: 178 us -> 111 us
  blocking collectives: 43.3 us -> 98.3 us
  matrix products: 21.4 us -> 15.8 us
    reduce_scatter x1 -> x0, waiting for transfers between devices: 76.7 us -> none  [per_device(): lax.psum_scatter(partial_value.astype(jnp.bfloat16), 'group', scatter_dim...]
    all_to_all x0 -> x1, blocking collectives: none -> 55 us  [per_device(): down_cols = lax.all_to_all(down_weight[0], 'group', 1, 0, tiled=True)]
    all_gather x0 -> x1, waiting for transfers between devices: none -> 9.22 us  [per_device(): hidden_all = lax.all_gather(hidden, 'group', axis=1, tiled=True)]
    dot_general x1 -> x2, matrix products: 13.5 us -> 8.46 us  [the longest x1 4.49 us: per_device(): lax.dot_general(row_block, up_weight[0], (((1,), (1,)), ((), ())), prefer...]
  transfers between devices with their start and end apart: 3 -> 3, of which waited for: 3 -> 3; matrix products, arithmetic and copies ran while one was open for 0% -> 1% of each run, Pallas kernels for 0% -> 0%
where the time goes in v3:
time: 262 us; the launch traced here: 261 us
  waiting for transfers between devices  111 us (42%)
  blocking collectives  98.3 us (38%)
  matrix products  15.8 us (6%)
  between operations  13.5 us (5%)
  starting transfers between devices  12.5 us (5%)
  local copies, waits for them, and re-layouts  7.35 us (3%)
  other arithmetic  3.17 us (1%)
    all_gather x1, waiting for transfers between devices, per_device(): row_block = lax.all_gather(arrived, 'group', axis=1, tiled=True)  73.5 us
    all_to_all x1, blocking collectives, per_device(): down_cols = lax.all_to_all(down_weight[0], 'group', 1, 0, tiled=True)  55 us
    all_to_all x1, blocking collectives, per_device(): lax.all_to_all(placed.reshape(experts, capacity, tokens.shape[1]), 'exper...  43.3 us
    all_to_all x1, waiting for transfers between devices, per_device(): lax.all_to_all(partial_value.astype(jnp.bfloat16).reshape(experts, capaci...  27.9 us
    all_to_all x1, starting transfers between devices, per_device(): lax.all_to_all(partial_value.astype(jnp.bfloat16).reshape(experts, capaci...  12.4 us
    all_gather x1, waiting for transfers between devices, per_device(): hidden_all = lax.all_gather(hidden, 'group', axis=1, tiled=True)  9.22 us
  transfers between devices with their start and end apart: 3, of which 3 were waited for; matrix products, arithmetic and copies ran while one was open for 1% of the time, Pallas kernels for 0%

profile of v3, /device:TPU:1, one launch (start us, length us, event | category | flops | bytes accessed | tf_op | source)
XLA Modules:
  0.0 261.2 jit_solution(7376772480139769284)
XLA Ops:
  6.5 0.0 copy-start
  6.5 0.0 all-gather.3.cloned.1.call-start
  6.5 0.9 copy.36
  7.4 0.1 eq.42
  7.5 0.1 eq.38
  7.6 1.2 reduce-window.6
  8.8 0.2 slice_reduce_fusion
  9.1 0.1 fusion.13
  9.2 0.1 reshape.40
  9.3 0.1 copy.39
  9.4 0.7 multiply_add_fusion
  10.1 0.1 copy.40
  10.2 0.5 fusion.4
  10.7 1.3 convolution_convert_fusion
  12.0 0.2 reshape.41
  12.2 43.3 %all_to_all.29 = bf16[64,12,512]{2,1,0:T(8,128)(2,1)} all-to-all(bf16[64,12,512]{2,1,0:T(8,128)(2,1)S(1)} %reshape.41), channel_id=1, replica_groups=mesh['expert'=64,'group'=8] {'expert'}, dimensions={0} | all-to-all | bytes 1572864 | tf_op jit(solution)/shard_map/all_to_all | solution.py:30
  55.4 2.1 reshape.42
  57.5 0.0 all-gather.3.cloned.1.call-update
  57.5 0.0 all-gather.5.cloned.1.call-start
  57.6 73.5 %all-gather.3.cloned.1.call-done = bf16[768,4096]{1,0:T(8,128)(2,1)} async-done(((bf16[768,512]{1,0:T(8,128)(2,1)}), bf16[768,4096]{1,0:T(8,128)(2,1)}) %all-gather.3.cloned.1.call-update) | async-done | bytes 6291472 | tf_op jit(solution)/shard_map/all_gather | solution.py:33
  131.1 0.0 copy-done
  131.1 0.0 copy-start.3
  131.1 5.2 %fusion.2 = f32[768,192]{0,1:T(8,128)S(1)} fusion(bf16[768,4096]{1,0:T(8,128)(2,1)} %all-gather.3.cloned.1.call-done, bf16[1,192,4096]{2,1,0:T(8,128)(2,1)S(1)} %copy-done), kind=kOutput, calls=%fused_computation.2 | convolution fusion | flops 1207959552 | bytes 8454144 | tf_op jit(solution)/shard_map/dot_general | solution.py:34
  136.3 0.0 copy-done.3
  136.3 0.0 copy-start.1
  136.3 4.5 %fusion.8 = bf16[768,192]{0,1:T(8,128)(2,1)} fusion(bf16[768,4096]{1,0:T(8,128)(2,1)S(1)} %copy-done.3, bf16[1,192,4096]{2,1,0:T(8,128)(2,1)} %param.8, f32[768,192]{0,1:T(8,128)S(1)} %fusion.2), kind=kOutput, calls=%fused_computation.10 | convolution fusion | flops 1208844288 | bytes 8749056 | tf_op jit(solution)/shard_map/dot_general | solution.py:37
  140.8 0.0 all-gather.5.cloned.1.call-update
  140.8 0.0 copy-done.1
  140.8 0.6 copy.44
  141.5 0.5 copy.42
  142.0 55.0 %all_to_all.30 = bf16[192,8,512]{2,0,1:T(8,128)(2,1)S(1)} all-to-all(bf16[192,8,512]{2,0,1:T(8,128)(2,1)S(1)} %copy.42), channel_id=1, replica_groups=mesh['expert'=64,'group'=8] {'group'}, dimensions={1} | all-to-all | bytes 3145728 | tf_op jit(solution)/shard_map/all_to_all | solution.py:42
  197.0 9.2 %all-gather.5.cloned.1.call-done = bf16[768,1536]{0,1:T(8,128)(2,1)} async-done(((bf16[768,192]{0,1:T(8,128)(2,1)}), bf16[768,1536]{0,1:T(8,128)(2,1)}) %all-gather.5.cloned.1.call-update) | async-done | bytes 2359312 | tf_op jit(solution)/shard_map/all_gather | solution.py:41
  206.2 4.0 %convolution_convert_fusion.1 = bf16[768,512]{1,0:T(8,128)(2,1)} fusion(bf16[768,1536]{0,1:T(8,128)(2,1)} %all-gather.5.cloned.1.call-done, bf16[1536,512]{1,0:T(8,128)(2,1)S(1)} %bitcast.45), kind=kOutput, calls=%fused_computation.8 | convolution fusion | flops 1208352768 | bytes 4718592 | tf_op jit(solution)/shard_map/dot_general | solution.py:43
  210.2 0.0 copy-start.2
  210.2 2.1 reshape.43
  212.3 12.4 %all-to-all-start.2 = ((bf16[64,12,512]{2,1,0:T(8,128)(2,1)}), bf16[64,12,512]{2,1,0:T(8,128)(2,1)S(1)}, u32[]{:S(2)}, u32[]{:S(2)}) async-start(bf16[64,12,512]{2,1,0:T(8,128)(2,1)} %reshape.43), calls=%async_computation.2 | async-start | bytes 2097152 | tf_op jit(solution)/shard_map/all_to_all | solution.py:44
  224.7 0.0 copy-done.2
  224.8 0.1 copy.41
  224.8 0.6 select_reduce_fusion
  225.4 27.9 %all-to-all-done.2 = bf16[64,12,512]{2,1,0:T(8,128)(2,1)S(1)} async-done(((bf16[64,12,512]{2,1,0:T(8,128)(2,1)}), bf16[64,12,512]{2,1,0:T(8,128)(2,1)S(1)}, u32[]{:S(2)}, u32[]{:S(2)}) %all-to-all-start.2) | async-done | bytes 786464 | tf_op jit(solution)/shard_map/all_to_all | solution.py:44
  253.3 0.2 reshape.44
  253.4 0.9 convolution_convert_fusion.2
  (3 shorter events, 0.1 us)
Async XLA Ops:
  6.5 124.6 %copy-start = (bf16[1,192,4096]{2,1,0:T(8,128)(2,1)S(1)}, bf16[1,192,4096]{2,1,0:T(8,128)(2,1)}, u32[]{:S(2)}) copy-start(bf16[1,192,4096]{2,1,0:T(8,128)(2,1)} %param.7) | copy-start | bytes 4718596
  6.5 124.6 %all-gather.3.cloned.1.call-start = ((), (), s32[]{:S(2)}) async-start(), calls=%async_computation.3 | async-start | bytes 7077888 | tf_op jit(solution)/shard_map/all_gather | solution.py:33
  57.5 148.7 %all-gather.5.cloned.1.call-start = ((), (), s32[]{:S(2)}) async-start(), calls=%async_computation.4 | async-start | bytes 2654208 | tf_op jit(solution)/shard_map/all_gather | solution.py:41
  131.1 5.2 %copy-start.3 = (bf16[768,4096]{1,0:T(8,128)(2,1)S(1)}, bf16[768,4096]{1,0:T(8,128)(2,1)}, u32[]{:S(2)}) copy-start(bf16[768,4096]{1,0:T(8,128)(2,1)} %all-gather.3.cloned.1.call-done) | copy-start | bytes 18874372
  136.3 4.5 %copy-start.1 = (bf16[1,192,4096]{2,1,0:T(8,128)(2,1)S(1)}, bf16[1,192,4096]{2,1,0:T(8,128)(2,1)}, u32[]{:S(2)}) copy-start(bf16[1,192,4096]{2,1,0:T(8,128)(2,1)} %param.9) | copy-start | bytes 4718596
  210.2 14.6 %copy-start.2 = (bf16[64,8]{0,1:T(8,128)(2,1)S(1)}, bf16[64,8]{0,1:T(8,128)(2,1)}, u32[]{:S(2)}) copy-start(bf16[64,8]{0,1:T(8,128)(2,1)} %param.11) | copy-start | bytes 3076
  212.3 41.0 %all-to-all-start.2 = ((bf16[64,12,512]{2,1,0:T(8,128)(2,1)}), bf16[64,12,512]{2,1,0:T(8,128)(2,1)S(1)}, u32[]{:S(2)}, u32[]{:S(2)}) async-start(bf16[64,12,512]{2,1,0:T(8,128)(2,1)} %reshape.43), calls=%async_computation.2 | async-start | bytes 2097152 | tf_op jit(solution)/shard_map/all_to_all | solution.py:44
Sparse Core Ops, SparseCore 0:
  57.7 73.4 all-gather.2
  140.9 65.2 all-gather.4

commit v4 on v3

--- a/solution.py
+++ b/solution.py
@@ -21,7 +21,7 @@
     return capacity, selector, weights
 
 
-def per_device(tokens, gate_weight, up_weight, down_weight, expert_ids, gate_scores):
+def layer(tokens, gate_weight, up_weight, down_weight, expert_ids, gate_scores):
     experts = lax.axis_size("expert")
     capacity, selector, weights = route_tables(expert_ids, gate_scores, experts)
     placed = lax.dot_general(
@@ -31,6 +31,7 @@
         placed.reshape(experts, capacity, tokens.shape[1]), "expert", 0, 0, tiled=True
     ).reshape(experts * capacity, tokens.shape[1])
     row_block = lax.all_gather(arrived, "group", axis=1, tiled=True)
+    down_cols = lax.all_to_all(down_weight[0], "group", 1, 0, tiled=True)
     gate_value = lax.dot_general(
         row_block, gate_weight[0], (((1,), (1,)), ((), ())), preferred_element_type=jnp.float32
     )
@@ -38,12 +39,19 @@
         row_block, up_weight[0], (((1,), (1,)), ((), ())), preferred_element_type=jnp.float32
     )
     hidden = (jax.nn.silu(gate_value) * up_value).astype(jnp.bfloat16)
-    hidden_all = lax.all_gather(hidden, "group", axis=1, tiled=True)
-    down_cols = lax.all_to_all(down_weight[0], "group", 1, 0, tiled=True)
-    partial_value = jnp.dot(hidden_all, down_cols, preferred_element_type=jnp.float32)
-    returned = lax.all_to_all(
-        partial_value.astype(jnp.bfloat16).reshape(experts, capacity, -1), "expert", 0, 0, tiled=True
-    ).reshape(experts * capacity, -1)
+    slots = hidden.reshape(experts, capacity, hidden.shape[1])
+    cut = capacity // 2
+    pieces = []
+    for c in range(2):
+        part = slots[:, c * cut:(c + 1) * cut].reshape(experts * cut, hidden.shape[1])
+        hidden_all = lax.all_gather(part, "group", axis=1, tiled=True)
+        partial_value = jnp.dot(hidden_all, down_cols, preferred_element_type=jnp.float32)
+        pieces.append(
+            lax.all_to_all(
+                partial_value.astype(jnp.bfloat16).reshape(experts, cut, -1), "expert", 0, 0, tiled=True
+            )
+        )
+    returned = jnp.concatenate(pieces, axis=1).reshape(experts * capacity, -1)
     combined = jnp.dot(weights, returned, preferred_element_type=jnp.float32)
     return combined.astype(jnp.bfloat16)
 
@@ -58,5 +66,5 @@
         P("expert", None),
     )
     return jax.shard_map(
-        per_device, mesh=mesh, in_specs=placed, out_specs=P("expert", "group"), check_vma=False
+        layer, mesh=mesh, in_specs=placed, out_specs=P("expert", "group"), check_vma=False
     )

time: 262 us -> 281 us (1.073)
  blocking collectives: 98.3 us -> 43.3 us
  waiting for transfers between devices: 111 us -> 161 us
  starting transfers between devices: 12.5 us -> 30.3 us
  local copies, waits for them, and re-layouts: 7.35 us -> 13.5 us
    all_to_all x2 -> x1, blocking collectives: 98.3 us -> 43.3 us  [layer(): lax.all_to_all(placed.reshape(experts, capacity, tokens.shape[1]), 'exper...]
    all_to_all x1 -> x3, waiting for transfers between devices: 27.9 us -> 65.5 us  [the longest x1 48.9 us: layer(): down_cols = lax.all_to_all(down_weight[0], 'group', 1, 0, tiled=True)]
    all_to_all x1 -> x3, starting transfers between devices: 12.4 us -> 30.2 us  [the longest x2 26 us: layer(): lax.all_to_all(partial_value.astype(jnp.bfloat16).reshape(experts, cut, -...]
    all_gather x2 -> x3, waiting for transfers between devices: 82.7 us -> 95.8 us  [the longest x1 73.5 us: layer(): row_block = lax.all_gather(arrived, 'group', axis=1, tiled=True)]
    reshape x4 -> x10, local copies, waits for them, and re-layouts: 4.56 us -> 7.81 us  [the longest x4 3.42 us: layer(): slots[:, c * cut:(c + 1) * cut].reshape(experts * cut, hidden.shape[1])]
    dot_general x5 -> x6, matrix products: 15.8 us -> 13.7 us  [the longest x1 5.15 us: layer(): lax.dot_general(row_block, gate_weight[0], (((1,), (1,)), ((), ())), pref...]
  transfers between devices with their start and end apart: 3 -> 6, of which waited for: 3 -> 4; matrix products, arithmetic and copies ran while one was open for 1% -> 5% of each run, Pallas kernels for 0% -> 0%
where the time goes in v4:
time: 281 us; the launch traced here: 280 us
  waiting for transfers between devices  161 us (57%)
  blocking collectives  43.3 us (15%)
  starting transfers between devices  30.3 us (11%)
  matrix products  13.7 us (5%)
  local copies, waits for them, and re-layouts  13.5 us (5%)
  between operations  13.3 us (5%)
  other arithmetic  4.58 us (2%)
    all_gather x1, waiting for transfers between devices, layer(): row_block = lax.all_gather(arrived, 'group', axis=1, tiled=True)  73.5 us
    all_to_all x1, waiting for transfers between devices, layer(): down_cols = lax.all_to_all(down_weight[0], 'group', 1, 0, tiled=True)  48.9 us
    all_to_all x1, blocking collectives, layer(): lax.all_to_all(placed.reshape(experts, capacity, tokens.shape[1]), 'exper...  43.3 us
    all_to_all x2, starting transfers between devices, layer(): lax.all_to_all(partial_value.astype(jnp.bfloat16).reshape(experts, cut, -...  26 us
    all_gather x2, waiting for transfers between devices, layer(): hidden_all = lax.all_gather(part, 'group', axis=1, tiled=True)  22.2 us
    all_to_all x2, waiting for transfers between devices, layer(): lax.all_to_all(partial_value.astype(jnp.bfloat16).reshape(experts, cut, -...  16.6 us
  transfers between devices with their start and end apart: 6, of which 4 were waited for; matrix products, arithmetic and copies ran while one was open for 5% of the time, Pallas kernels for 0%

profile of v4, /device:TPU:1, one launch (start us, length us, event | category | flops | bytes accessed | tf_op | source)
XLA Modules:
  0.0 279.9 jit_solution(4807758236489379307)
XLA Ops:
  6.5 0.0 copy-start
  6.5 0.0 all-gather.4.cloned.1.call-start
  6.5 0.9 copy.44
  7.4 0.1 eq.42
  7.5 0.1 eq.38
  7.6 1.2 reduce-window.6
  8.8 0.2 slice_reduce_fusion
  9.1 0.1 fusion.13
  9.2 0.1 reshape.52
  9.3 0.1 copy.47
  9.4 0.7 multiply_add_fusion
  10.1 0.1 copy.48
  10.2 0.0 copy-start.1
  10.2 0.5 fusion.4
  10.7 0.1 copy-done.1
  10.8 1.3 convolution_convert_fusion
  12.1 0.2 reshape.53
  12.2 43.3 %all_to_all.34 = bf16[64,12,512]{2,1,0:T(8,128)(2,1)} all-to-all(bf16[64,12,512]{2,1,0:T(8,128)(2,1)S(1)} %reshape.53), channel_id=1, replica_groups=mesh['expert'=64,'group'=8] {'expert'}, dimensions={0} | all-to-all | bytes 1572864 | tf_op jit(solution)/shard_map/all_to_all | solution.py:30
  55.5 2.1 reshape.54
  57.6 0.0 all-gather.4.cloned.1.call-update
  57.6 0.0 copy-start.5
  57.6 0.0 all-gather.6.cloned.1.call-start
  57.6 73.5 %all-gather.4.cloned.1.call-done = bf16[768,4096]{1,0:T(8,128)(2,1)} async-done(((bf16[768,512]{1,0:T(8,128)(2,1)}), bf16[768,4096]{1,0:T(8,128)(2,1)}) %all-gather.4.cloned.1.call-update) | async-done | bytes 6291472 | tf_op jit(solution)/shard_map/all_gather | solution.py:33
  131.2 0.0 copy-done
  131.2 0.0 copy-start.4
  131.2 5.2 %fusion.2 = f32[768,192]{0,1:T(8,128)S(1)} fusion(bf16[768,4096]{1,0:T(8,128)(2,1)} %all-gather.4.cloned.1.call-done, bf16[1,192,4096]{2,1,0:T(8,128)(2,1)S(1)} %copy-done), kind=kOutput, calls=%fused_computation.2 | convolution fusion | flops 1207959552 | bytes 8454144 | tf_op jit(solution)/shard_map/dot_general | solution.py:35
  136.3 0.0 copy-done.5
  136.3 0.0 copy-done.4
  136.3 2.2 fusion.8
  138.6 0.2 copy.50
  138.7 0.1 reshape.55
  138.9 0.1 fusion.16
  139.0 0.1 reshape.56
  139.1 0.8 copy.51
  139.9 0.0 all-gather.6.cloned.1.call-update
  139.9 2.1 copy.55
  141.9 1.7 copy.52
  143.6 4.2 %all-to-all-start.1 = ((bf16[192,8,512]{2,0,1:T(8,128)(2,1)}), bf16[192,8,512]{2,0,1:T(8,128)(2,1)S(1)}, u32[]{:S(2)}, u32[]{:S(2)}) async-start(bf16[192,8,512]{2,0,1:T(8,128)(2,1)} %copy.52), calls=%async_computation.1 | async-start | bytes 3145728 | tf_op jit(solution)/shard_map/all_to_all | solution.py:34
  147.8 0.0 all-gather.8.cloned.1.call-start
  147.8 0.8 reshape.58
  148.7 1.7 copy.53
  150.4 0.0 all-gather.8.cloned.1.call-update
  150.4 48.9 %all-to-all-done.1 = bf16[192,8,512]{2,0,1:T(8,128)(2,1)S(1)} async-done(((bf16[192,8,512]{2,0,1:T(8,128)(2,1)}), bf16[192,8,512]{2,0,1:T(8,128)(2,1)S(1)}, u32[]{:S(2)}, u32[]{:S(2)}) %all-to-all-start.1) | async-done | bytes 1572896 | tf_op jit(solution)/shard_map/all_to_all | solution.py:34
  199.3 0.0 all-gather.6.cloned.1.call-done
  199.3 2.1 convolution_convert_fusion.2
  201.4 0.9 reshape.57
  202.3 11.0 %all-to-all-start.2 = ((bf16[64,6,512]{2,1,0:T(8,128)(2,1)}), bf16[64,6,512]{2,1,0:T(8,128)(2,1)}, u32[]{:S(2)}, u32[]{:S(2)}) async-start(bf16[64,6,512]{2,1,0:T(8,128)(2,1)} %reshape.57), calls=%async_computation.2 | async-start | bytes 1048576 | tf_op jit(solution)/shard_map/all_to_all | solution.py:50
  213.3 22.2 %all-gather.8.cloned.1.call-done = bf16[384,1536]{0,1:T(8,128)(2,1)} async-done(((bf16[384,192]{0,1:T(8,128)(2,1)}), bf16[384,1536]{0,1:T(8,128)(2,1)}) %all-gather.8.cloned.1.call-update) | async-done | bytes 1179664 | tf_op jit(solution)/shard_map/all_gather | solution.py:47
  235.6 2.1 convolution_convert_fusion.1
  237.7 0.0 copy-start.3
  237.7 0.0 copy-start.2
  237.7 0.9 reshape.59
  238.6 0.0 all-to-all-done.2
  238.6 15.0 %all-to-all-start.3 = ((bf16[64,6,512]{2,1,0:T(8,128)(2,1)}), bf16[64,6,512]{2,1,0:T(8,128)(2,1)S(1)}, u32[]{:S(2)}, u32[]{:S(2)}) async-start(bf16[64,6,512]{2,1,0:T(8,128)(2,1)} %reshape.59), calls=%async_computation.3 | async-start | bytes 1048576 | tf_op jit(solution)/shard_map/all_to_all | solution.py:50
  253.6 0.0 copy-done.3
  253.6 0.1 copy.49
  253.7 0.0 copy-done.2
  253.7 0.6 select_reduce_fusion
  254.3 16.6 %all-to-all-done.3 = bf16[64,6,512]{2,1,0:T(8,128)(2,1)S(1)} async-done(((bf16[64,6,512]{2,1,0:T(8,128)(2,1)}), bf16[64,6,512]{2,1,0:T(8,128)(2,1)S(1)}, u32[]{:S(2)}, u32[]{:S(2)}) %all-to-all-start.3) | async-done | bytes 393248 | tf_op jit(solution)/shard_map/all_to_all | solution.py:50
  270.9 1.4 pad_maximum_fusion
  272.3 0.2 reshape.60
  272.5 0.9 convolution_convert_fusion.3
  (3 shorter events, 0.1 us)
Async XLA Ops:
  6.5 124.6 %copy-start = (bf16[1,192,4096]{2,1,0:T(8,128)(2,1)S(1)}, bf16[1,192,4096]{2,1,0:T(8,128)(2,1)}, u32[]{:S(2)}) copy-start(bf16[1,192,4096]{2,1,0:T(8,128)(2,1)} %param.7) | copy-start | bytes 4718596
  6.5 124.6 %all-gather.4.cloned.1.call-start = ((), (), s32[]{:S(2)}) async-start(), calls=%async_computation.4 | async-start | bytes 7077888 | tf_op jit(solution)/shard_map/all_gather | solution.py:33
  10.2 0.6 copy-start.1
  57.6 78.7 %copy-start.5 = (bf16[1,192,4096]{2,1,0:T(8,128)(2,1)S(1)}, bf16[1,192,4096]{2,1,0:T(8,128)(2,1)}, u32[]{:S(2)}) copy-start(bf16[1,192,4096]{2,1,0:T(8,128)(2,1)} %param.8) | copy-start | bytes 4718596
  57.6 141.7 %all-gather.6.cloned.1.call-start = ((), (), s32[]{:S(2)}) async-start(), calls=%async_computation.5 | async-start | bytes 1327104 | tf_op jit(solution)/shard_map/all_gather | solution.py:47
  131.2 5.2 %copy-start.4 = (bf16[768,4096]{1,0:T(8,128)(2,1)S(1)}, bf16[768,4096]{1,0:T(8,128)(2,1)}, u32[]{:S(2)}) copy-start(bf16[768,4096]{1,0:T(8,128)(2,1)} %all-gather.4.cloned.1.call-done) | copy-start | bytes 18874372
  143.6 55.7 %all-to-all-start.1 = ((bf16[192,8,512]{2,0,1:T(8,128)(2,1)}), bf16[192,8,512]{2,0,1:T(8,128)(2,1)S(1)}, u32[]{:S(2)}, u32[]{:S(2)}) async-start(bf16[192,8,512]{2,0,1:T(8,128)(2,1)} %copy.52), calls=%async_computation.1 | async-start | bytes 3145728 | tf_op jit(solution)/shard_map/all_to_all | solution.py:34
  147.8 87.8 %all-gather.8.cloned.1.call-start = ((), (), s32[]{:S(2)}) async-start(), calls=%async_computation.6 | async-start | bytes 1327104 | tf_op jit(solution)/shard_map/all_gather | solution.py:47
  202.3 36.3 %all-to-all-start.2 = ((bf16[64,6,512]{2,1,0:T(8,128)(2,1)}), bf16[64,6,512]{2,1,0:T(8,128)(2,1)}, u32[]{:S(2)}, u32[]{:S(2)}) async-start(bf16[64,6,512]{2,1,0:T(8,128)(2,1)} %reshape.57), calls=%async_computation.2 | async-start | bytes 1048576 | tf_op jit(solution)/shard_map/all_to_all | solution.py:50
  237.7 16.0 %copy-start.3 = (bf16[64,8]{0,1:T(8,128)(2,1)S(1)}, bf16[64,8]{0,1:T(8,128)(2,1)}, u32[]{:S(2)}) copy-start(bf16[64,8]{0,1:T(8,128)(2,1)} %param.11) | copy-start | bytes 3076
  237.7 16.1 %copy-start.2 = (s32[64,8]{1,0:T(8,128)S(1)}, s32[64,8]{1,0:T(8,128)}, u32[]{:S(2)}) copy-start(s32[64,8]{1,0:T(8,128)} %copy-done.1) | copy-start | bytes 6148
  238.6 32.3 %all-to-all-start.3 = ((bf16[64,6,512]{2,1,0:T(8,128)(2,1)}), bf16[64,6,512]{2,1,0:T(8,128)(2,1)S(1)}, u32[]{:S(2)}, u32[]{:S(2)}) async-start(bf16[64,6,512]{2,1,0:T(8,128)(2,1)} %reshape.59), calls=%async_computation.3 | async-start | bytes 1048576 | tf_op jit(solution)/shard_map/all_to_all | solution.py:50
Sparse Core Ops, SparseCore 0:
  57.7 73.4 all-gather.3
  140.0 53.7 all-gather.5
  195.9 39.6 all-gather.7
